TPU v7x, 256 devices: a whole 4x4x8 slice. The times are simulated.
256 devices in a mesh: layer: 2 (over core), feat: 4 (over x), tok: 32 (over z, y).
Axes of the slice: x: 4, y: 4, z: 8, core: 2. Of those that a mesh axis runs over, the one named last changes fastest.
Arguments:
- resid_in: bfloat16 [8192, 2304], P('tok', 'feat'), may hold values from -6 to 6
- attn_out: bfloat16 [2, 8192, 2304], P('layer', 'tok', 'feat'), may hold values from -4 to 4
- carry_in: bfloat16 [8192, 2304], P('tok', 'feat'), may hold values from -4 to 4
- enc_weight: bfloat16 [2, 2304, 8192], P('layer', None, 'feat'), may hold values from -0.125 to 0.125
- enc_bias: float32 [2, 8192], P('layer', 'feat'), may hold values from -3 to 3
- dec_own: bfloat16 [2, 8192, 2304], P('layer', 'feat', 'tok'), may hold values from -0.125 to 0.125
- dec_next: bfloat16 [2, 8192, 2304], P('layer', 'feat', 'tok'), may hold values from -0.125 to 0.125
- block_list: int32 [2, 64, 32], P('layer', 'tok'), may hold values from 0 to 63, all different within a row
- block_count: int32 [2, 64], P('layer', 'tok'), may hold values from 8 to 32, as said below
Outputs:
- reconstruction: bfloat16 [2, 8192, 2304], P('layer', 'tok', 'feat')
- outgoing: bfloat16 [2, 8192, 2304], P('layer', 'tok', 'feat')
Inputs may be any that keep to these rules, and one draw needn't show every extreme that they name: Each row of block_list names 32 different blocks; only its first block_count entries are in use. `block_count`: some entry equals 32.
All inputs are finite; a program needn't handle non-finite values.
Results may differ from a plain program's by a relative error of at most 0.015.
Values may be sent and summed in bfloat16 or wider, within the bound.
No kernel may reach another device: no remote copies, remote signals or barrier semaphores. Data moves between devices by JAX's collectives and lax.ppermute only.
A program may use at most 128 MiB of HBM per device.

v0:
```python
import jax
import jax.numpy as jnp
from jax import lax
from jax.sharding import PartitionSpec as P

BLOCK = 128
TILE = 128


def from_behind(shard, axis, by):
    length = lax.axis_size(axis)
    pairs = [(i, i + by) for i in range(length) if 0 <= i + by < length]
    return lax.ppermute(shard, axis, pairs)


def block_mask(block_list, block_count, tile_index, feat_index, blocks_dev):
    listed = lax.dynamic_index_in_dim(block_list[0], tile_index, 0, keepdims=False)
    count_now = lax.dynamic_index_in_dim(block_count[0], tile_index, 0, keepdims=False)
    in_use = jnp.arange(listed.shape[0], dtype=jnp.int32) < count_now
    own_blocks = feat_index * blocks_dev + jnp.arange(blocks_dev, dtype=jnp.int32)
    matches = (listed[None, :] == own_blocks[:, None]) & in_use[None, :]
    return jnp.any(matches, axis=1)


def decode_every(gathered, enc_weight, enc_bias, decoders, active):
    preact = (
        jnp.dot(gathered, enc_weight[0], preferred_element_type=jnp.float32) + enc_bias[0][None, :]
    )
    feat_mask = jnp.repeat(active.astype(jnp.float32), BLOCK)
    features = (jax.nn.relu(preact) * feat_mask[None, :]).astype(jnp.bfloat16)
    own_part = jnp.dot(features, decoders[0], preferred_element_type=jnp.float32)
    next_part = jnp.dot(features, decoders[1], preferred_element_type=jnp.float32)
    return jnp.stack([own_part, next_part])


def store_rows(holder, values, row_start, is_valid):
    previous = lax.dynamic_slice_in_dim(holder, row_start, values.shape[0], 0)
    return lax.dynamic_update_slice_in_dim(
        holder, jnp.where(is_valid, values, previous), row_start, 0
    )


def shards(
    resid_in, attn_out, carry_in, enc_weight, enc_bias, dec_own, dec_next, block_list, block_count
):
    layer_count = lax.axis_size("layer")
    section_index = lax.axis_index("layer")
    feat_index = lax.axis_index("feat")
    tile_count = block_count.shape[1]
    columns = resid_in.shape[1]
    blocks_dev = enc_weight.shape[2] // BLOCK
    decoders = (
        lax.all_gather(dec_own[0], "tok", axis=1, tiled=True),
        lax.all_gather(dec_next[0], "tok", axis=1, tiled=True),
    )
    empty_rows = jnp.zeros((resid_in.shape[0], columns), jnp.bfloat16)
    nothing_yet = jnp.zeros((2, TILE, columns), jnp.bfloat16)

    def advance(step_index, state_tuple):
        arrived, recon_holder, outgoing_holder = state_tuple
        tile_index = step_index - section_index
        is_valid = (tile_index >= 0) & (tile_index < tile_count)
        tile_index = jnp.clip(tile_index, 0, tile_count - 1)
        row_start = tile_index * TILE
        first_section = section_index == 0
        residual = jnp.where(
            first_section, lax.dynamic_slice_in_dim(resid_in, row_start, TILE, 0), arrived[0]
        )
        incoming = jnp.where(
            first_section, lax.dynamic_slice_in_dim(carry_in, row_start, TILE, 0), arrived[1]
        )
        gathered = lax.all_gather(residual, "feat", axis=1, tiled=True)
        active = block_mask(block_list, block_count, tile_index, feat_index, blocks_dev)
        zero_terms = jnp.zeros((2, TILE, gathered.shape[1]), jnp.float32)
        terms = lax.cond(
            is_valid,
            lambda source: decode_every(source, enc_weight, enc_bias, decoders, active),
            lambda source: zero_terms,
            gathered,
        )
        summed = lax.psum_scatter(
            terms.astype(jnp.bfloat16), "feat", scatter_dimension=2, tiled=True
        ).astype(jnp.float32)
        attention = lax.dynamic_slice_in_dim(attn_out[0], row_start, TILE, 0)
        recon_now = summed[0] + incoming.astype(jnp.float32)
        new_residual = (
            residual.astype(jnp.float32) + attention.astype(jnp.float32) + recon_now
        ).astype(jnp.bfloat16)
        outgoing_now = summed[1].astype(jnp.bfloat16)
        recon_holder = store_rows(recon_holder, recon_now.astype(jnp.bfloat16), row_start, is_valid)
        outgoing_holder = store_rows(outgoing_holder, outgoing_now, row_start, is_valid)
        arrived = from_behind(jnp.stack([new_residual, outgoing_now]), "layer", 1)
        return (arrived, recon_holder, outgoing_holder)

    finished = lax.fori_loop(
        0, tile_count + layer_count - 1, advance, (nothing_yet, empty_rows, empty_rows)
    )
    return (finished[1][None], finished[2][None])


def solution(mesh):
    return jax.shard_map(
        shards,
        mesh=mesh,
        in_specs=(
            P("tok", "feat"),
            P("layer", "tok", "feat"),
            P("tok", "feat"),
            P("layer", None, "feat"),
            P("layer", "feat"),
            P("layer", "feat", "tok"),
            P("layer", "feat", "tok"),
            P("layer", "tok", None),
            P("layer", "tok"),
        ),
        out_specs=(P("layer", "tok", "feat"), P("layer", "tok", "feat")),
        check_vma=False,
    )
```

profile of v0, /device:TPU:1, one launch (start us, length us, event | category | flops | bytes accessed | tf_op | source)
XLA Modules:
  0.0 485.6 jit_solution(13964440871166911584)
XLA Ops:
  8.7 108.2 %all-gather.5.cloned.1.call-done = bf16[1,2048,2304]{1,2,0:T(8,128)(2,1)} async-done(((bf16[1,2048,72]{1,2,0:T(8,128)(2,1)}), bf16[1,2048,2304]{1,2,0:T(8,128)(2,1)}) %all-gather.5.cloned.1.call-update) | async-done | bytes 9437200 | tf_op jit(solution)/shard_map/all_gather | solution.py:53
  116.8 12.4 %copy.26 = bf16[2048,2304]{1,0:T(8,128)(2,1)} copy(bf16[2048,2304]{0,1:T(8,128)(2,1)} %bitcast.82) | data formatting | bytes 18874368 | tf_op jit(solution)/shard_map/while | solution.py:95
  129.2 90.5 %all-gather.7.cloned.1.call-done = bf16[1,2048,2304]{1,2,0:T(8,128)(2,1)} async-done(((bf16[1,2048,72]{1,2,0:T(8,128)(2,1)}), bf16[1,2048,2304]{1,2,0:T(8,128)(2,1)}) %all-gather.7.cloned.1.call-update) | async-done | bytes 9437200 | tf_op jit(solution)/shard_map/all_gather | solution.py:54
  219.8 12.8 %copy.27 = bf16[2048,2304]{1,0:T(8,128)(2,1)} copy(bf16[2048,2304]{0,1:T(8,128)(2,1)} %bitcast.83) | data formatting | bytes 18874368 | tf_op jit(solution)/shard_map/while | solution.py:95
  232.7 245.5 %while.19 = (s32[]{:T(128)}, bf16[2,128,576]{1,2,0:T(8,128)(2,1)S(1)}, bf16[256,576]{0,1:T(8,128)(2,1)S(1)}, bf16[256,576]{0,1:T(8,128)(2,1)S(1)}, pred[]{:T(512...) while((s32[]{:T(128)}, ...), condition=%wide.region_5.6_spmd, body=%wide.region_0.5_spmd.sunk | while | flops 3627509248 | bytes 116467488 | solution.py:95
  232.9 11.7 %all_gather.18 = bf16[128,2304]{0,1:T(8,128)(2,1)S(1)} all-gather(bf16[128,576]{0,1:T(8,128)(2,1)S(1)} %bitcast_select_fusion.4), channel_id=1, replica_groups=mesh['layer'=2,'feat'=4,'tok'=32] {'feat'}, dimensions={1}, use_global_device_ids=true | all-gather | bytes 737280 | tf_op jit(solution)/shard_map/while/body/eval_jaxpr/all_gather | solution.py:72
  244.7 2.7 copy.33
  248.7 59.4 %all-reduce.5.cloned.1.call-done = bf16[2,128,2304]{1,0,2:T(2,128)(2,1)} async-done(((bf16[2,128,2304]{1,0,2:T(2,128)(2,1)}), bf16[2,128,2304]{1,0,2:T(2,128)(2,1)}) %all-reduce.5.cloned.1.call-update) | async-done | bytes 1179664 | tf_op jit(solution)/shard_map/while
  308.0 1.2 constant_dynamic-slice_fusion.4
  309.6 1.3 collective-permute-start
  310.9 2.9 collective-permute-done
  313.8 10.9 %all_gather.18 = bf16[128,2304]{0,1:T(8,128)(2,1)S(1)} all-gather(bf16[128,576]{0,1:T(8,128)(2,1)S(1)} %bitcast_select_fusion.4), channel_id=1, replica_groups=mesh['layer'=2,'feat'=4,'tok'=32] {'feat'}, dimensions={1}, use_global_device_ids=true | all-gather | bytes 737280 | tf_op jit(solution)/shard_map/while/body/eval_jaxpr/all_gather | solution.py:72
  324.8 10.8 %conditional.2 = (bf16[2,128,2304]{2,1,0:T(8,128)(2,1)S(1)}) conditional(s32[]{:T(128)} %convert_element_type.137, () %tuple.76, (bf16[1,2304,2048]{2,1,0:T(8,128)(2,1)}, bf16[128,2304]{0,1:T(8,128)(2,1)S(1)}, f32[1,2048]{1,0:T(1,128)S(1)}, s32[1,2,32]{2,1,0:T(2,128)S(1)}, s32[]{:T(128)}, /*index=5*/s32[]{:T(128)}, s32[16,1]{0,1:T(1,128)S(1)}, ...), branch_computations={%region_1.1_spmd, %region_2.3_spmd} | conditional | flops 3625518592 | bytes 100099104 | solution.py:75
  325.4 0.9 compare_bitcast_fusion
  326.6 5.8 %fusion.11 = bf16[128,2048]{1,0:T(8,128)(2,1)S(1)} fusion(bf16[128,2304]{0,1:T(8,128)(2,1)S(1)} %get-tuple-element.503, bf16[1,2304,2048]{2,1,0:T(8,128)(2,1)} %get-tuple-element.426, f32[2048]{0:T(1024)S(1)} %broadcast_bitcast_fusion, f32[2048]{0:T(1024)S(1)} %bitcast.86), kind=kOutput, calls=%fused_computation.7 | convolution fusion | flops 1209008128 | bytes 10567680 | tf_op jit(solution)/shard_map/while/body/eval_jaxpr/cond/branch_1_fun/dot_general | solution.py:27
  332.5 1.4 convolution_bitcast_fusion
  334.0 1.4 convolution_bitcast_fusion.1
  335.6 2.7 copy.33
  339.5 52.4 %all-reduce.5.cloned.1.call-done = bf16[2,128,2304]{1,0,2:T(2,128)(2,1)} async-done(((bf16[2,128,2304]{1,0,2:T(2,128)(2,1)}), bf16[2,128,2304]{1,0,2:T(2,128)(2,1)}) %all-reduce.5.cloned.1.call-update) | async-done | bytes 1179664 | tf_op jit(solution)/shard_map/while
  391.9 1.2 constant_dynamic-slice_fusion.4
  393.5 1.3 collective-permute-start
  394.8 2.9 collective-permute-done
  397.7 10.9 %all_gather.18 = bf16[128,2304]{0,1:T(8,128)(2,1)S(1)} all-gather(bf16[128,576]{0,1:T(8,128)(2,1)S(1)} %bitcast_select_fusion.4), channel_id=1, replica_groups=mesh['layer'=2,'feat'=4,'tok'=32] {'feat'}, dimensions={1}, use_global_device_ids=true | all-gather | bytes 737280 | tf_op jit(solution)/shard_map/while/body/eval_jaxpr/all_gather | solution.py:72
  408.7 10.8 %conditional.2 = (bf16[2,128,2304]{2,1,0:T(8,128)(2,1)S(1)}) conditional(s32[]{:T(128)} %convert_element_type.137, () %tuple.76, (bf16[1,2304,2048]{2,1,0:T(8,128)(2,1)}, bf16[128,2304]{0,1:T(8,128)(2,1)S(1)}, f32[1,2048]{1,0:T(1,128)S(1)}, s32[1,2,32]{2,1,0:T(2,128)S(1)}, s32[]{:T(128)}, /*index=5*/s32[]{:T(128)}, s32[16,1]{0,1:T(1,128)S(1)}, ...), branch_computations={%region_1.1_spmd, %region_2.3_spmd} | conditional | flops 3625518592 | bytes 100099104 | solution.py:75
  410.5 5.8 %fusion.11 = bf16[128,2048]{1,0:T(8,128)(2,1)S(1)} fusion(bf16[128,2304]{0,1:T(8,128)(2,1)S(1)} %get-tuple-element.503, bf16[1,2304,2048]{2,1,0:T(8,128)(2,1)} %get-tuple-element.426, f32[2048]{0:T(1024)S(1)} %broadcast_bitcast_fusion, f32[2048]{0:T(1024)S(1)} %bitcast.86), kind=kOutput, calls=%fused_computation.7 | convolution fusion | flops 1209008128 | bytes 10567680 | tf_op jit(solution)/shard_map/while/body/eval_jaxpr/cond/branch_1_fun/dot_general | solution.py:27
  416.4 1.4 convolution_bitcast_fusion
  417.9 1.4 convolution_bitcast_fusion.1
  419.5 2.7 copy.33
  423.4 49.1 %all-reduce.5.cloned.1.call-done = bf16[2,128,2304]{1,0,2:T(2,128)(2,1)} async-done(((bf16[2,128,2304]{1,0,2:T(2,128)(2,1)}), bf16[2,128,2304]{1,0,2:T(2,128)(2,1)}) %all-reduce.5.cloned.1.call-update) | async-done | bytes 1179664 | tf_op jit(solution)/shard_map/while
  472.5 1.2 constant_dynamic-slice_fusion.4
  474.0 1.3 collective-permute-start
  475.3 2.9 collective-permute-done
  (90 shorter events, 8.8 us)
Async XLA Ops:
  7.2 109.7 %all-gather.5.cloned.1.call-start = ((), (), s32[]{:S(2)}) async-start(), calls=%async_computation | async-start | bytes 9732096 | tf_op jit(solution)/shard_map/all_gather | solution.py:53
  7.9 211.8 %all-gather.7.cloned.1.call-start = ((), (), s32[]{:S(2)}) async-start(), calls=%async_computation.1 | async-start | bytes 9732096 | tf_op jit(solution)/shard_map/all_gather | solution.py:54
  219.7 12.9 %copy-start.1 = (bf16[256,576]{0,1:T(8,128)(2,1)S(1)}, bf16[256,576]{0,1:T(8,128)(2,1)}, u32[]{:S(2)}) copy-start(bf16[256,576]{0,1:T(8,128)(2,1)} %param.15) | copy-start | bytes 884740
  219.7 13.0 %copy-start.4 = (bf16[1,256,576]{1,2,0:T(8,128)(2,1)S(1)}, bf16[1,256,576]{1,2,0:T(8,128)(2,1)}, u32[]{:S(2)}) copy-start(bf16[1,256,576]{1,2,0:T(8,128)(2,1)} %param.14) | copy-start | bytes 884740
  219.7 13.0 %copy-start.5 = (bf16[256,576]{0,1:T(8,128)(2,1)S(1)}, bf16[256,576]{0,1:T(8,128)(2,1)}, u32[]{:S(2)}) copy-start(bf16[256,576]{0,1:T(8,128)(2,1)} %param.13) | copy-start | bytes 884740
  219.7 13.0 %copy-start.6 = (f32[1,2048]{1,0:T(1,128)S(1)}, f32[1,2048]{1,0:T(1,128)}, u32[]{:S(2)}) copy-start(f32[1,2048]{1,0:T(1,128)} %param.17) | copy-start | bytes 24580
  219.7 13.0 %copy-start.7 = (s32[1,2,32]{2,1,0:T(2,128)S(1)}, s32[1,2,32]{2,1,0:T(2,128)}, u32[]{:S(2)}) copy-start(s32[1,2,32]{2,1,0:T(2,128)} %param.20) | copy-start | bytes 772
  219.7 13.0 %copy-start.8 = (s32[1,2]{1,0:T(1,128)S(1)}, s32[1,2]{1,0:T(1,128)}, u32[]{:S(2)}) copy-start(s32[1,2]{1,0:T(1,128)} %param.21) | copy-start | bytes 28
  219.7 13.0 %copy-start.9 = (u32[256]{0:T(256)S(1)}, u32[256]{0:T(256)}, u32[]{:S(2)}) copy-start(u32[256]{0:T(256)} %constant.151) | copy-start | bytes 3076
  232.7 75.3 %all-reduce.5.cloned.1.call-start = ((), (), s32[]{:S(2)}) async-start(), calls=%async_computation.2 | async-start | bytes 2359296 | tf_op jit(solution)/shard_map/while
  309.6 4.2 collective-permute-start
  313.8 78.2 %all-reduce.5.cloned.1.call-start = ((), (), s32[]{:S(2)}) async-start(), calls=%async_computation.2 | async-start | bytes 2359296 | tf_op jit(solution)/shard_map/while
  324.8 7.7 %copy-start = (bf16[2048,2304]{1,0:T(8,128)(2,1)S(1)}, bf16[2048,2304]{1,0:T(8,128)(2,1)}, u32[]{:S(2)}) copy-start(bf16[2048,2304]{1,0:T(8,128)(2,1)} %get-tuple-element.435) | copy-start | bytes 28311556 | tf_op jit(solution)/shard_map/while/body/eval_jaxpr/cond
  326.6 7.3 %slice-start = ((s8[9437184]{0:T(1024)(128)(4,1)}), s8[4194304]{0:T(1024)(128)(4,1)S(1)}, s32[]{:S(2)}) async-start(s8[9437184]{0:T(1024)(128)(4,1)} %bitcast.80), calls=%async_computation.3 | async-start | bytes 8388608 | tf_op jit(solution)/shard_map/while/body/eval_jaxpr/cond
  326.6 7.3 %slice-start.1 = ((s8[9437184]{0:T(1024)(128)(4,1)}), s8[4194304]{0:T(1024)(128)(4,1)S(1)}, s32[]{:S(2)}) async-start(s8[9437184]{0:T(1024)(128)(4,1)} %bitcast.80), calls=%async_computation.4 | async-start | bytes 8388608 | tf_op jit(solution)/shard_map/while/body/eval_jaxpr/cond
  332.5 1.5 slice-start.2
  393.5 4.2 collective-permute-start
  397.7 74.8 %all-reduce.5.cloned.1.call-start = ((), (), s32[]{:S(2)}) async-start(), calls=%async_computation.2 | async-start | bytes 2359296 | tf_op jit(solution)/shard_map/while
  408.7 7.7 %copy-start = (bf16[2048,2304]{1,0:T(8,128)(2,1)S(1)}, bf16[2048,2304]{1,0:T(8,128)(2,1)}, u32[]{:S(2)}) copy-start(bf16[2048,2304]{1,0:T(8,128)(2,1)} %get-tuple-element.435) | copy-start | bytes 28311556 | tf_op jit(solution)/shard_map/while/body/eval_jaxpr/cond
  410.5 7.3 %slice-start = ((s8[9437184]{0:T(1024)(128)(4,1)}), s8[4194304]{0:T(1024)(128)(4,1)S(1)}, s32[]{:S(2)}) async-start(s8[9437184]{0:T(1024)(128)(4,1)} %bitcast.80), calls=%async_computation.3 | async-start | bytes 8388608 | tf_op jit(solution)/shard_map/while/body/eval_jaxpr/cond
  410.5 7.3 %slice-start.1 = ((s8[9437184]{0:T(1024)(128)(4,1)}), s8[4194304]{0:T(1024)(128)(4,1)S(1)}, s32[]{:S(2)}) async-start(s8[9437184]{0:T(1024)(128)(4,1)} %bitcast.80), calls=%async_computation.4 | async-start | bytes 8388608 | tf_op jit(solution)/shard_map/while/body/eval_jaxpr/cond
  416.4 1.5 slice-start.2
  474.0 4.2 collective-permute-start
  478.3 0.7 copy-start.2
  478.3 0.8 copy-start.3
Sparse Core Ops, SparseCore 0:
  10.5 106.2 all-gather.4
  119.4 100.2 all-gather.6
  247.5 60.4 all-reduce.4
  338.4 53.4 all-reduce.4
  422.3 50.1 all-reduce.4
where the time goes:
time: 486 us
  waiting for transfers between devices  370 us (76%)
  local copies, waits for them, and re-layouts  41.3 us (8%)
  blocking collectives  33.6 us (7%)
  matrix products  17.4 us (4%)
  between operations  13.8 us (3%)
    while x6, waiting for transfers between devices  161 us
    all_gather x1, waiting for transfers between devices, shards(): lax.all_gather(dec_own[0], 'tok', axis=1, tiled=True)  108 us
    all_gather x1, waiting for transfers between devices, shards(): lax.all_gather(dec_next[0], 'tok', axis=1, tiled=True)  90.5 us
    all_gather x3, blocking collectives, advance(): gathered = lax.all_gather(residual, 'feat', axis=1, tiled=True)  33.6 us
    while x2, local copies, waits for them, and re-layouts, shards(): lax.fori_loop(0, tile_count + layer_count - 1, advance, (nothing_yet, emp...  25.2 us
    dot_general x2, matrix products, decode_every(): jnp.dot(gathered, enc_weight[0], preferred_element_type=jnp.float32)  11.7 us
  transfers between devices with their start and end apart: 8, of which 8 were waited for; matrix products, arithmetic and copies ran while one was open for 3% of the time, Pallas kernels for 0%

commit v1 on v0

--- a/solution.py
+++ b/solution.py
@@ -1,3 +1,4 @@
+import functools
 import jax
 import jax.numpy as jnp
 from jax import lax
@@ -5,6 +6,19 @@
 
 BLOCK = 128
 TILE = 128
+
+
+def wait_pages(field_in, dim_at):
+    return lax.all_to_all(
+        jnp.concatenate([field_in for _ in range(lax.axis_size("tok"))], dim_at),
+        "tok",
+        dim_at,
+        dim_at,
+        tiled=True,
+    )
+
+
+meet_surface_over_axis = functools.partial(wait_pages, dim_at=1)
 
 
 def from_behind(shard, axis, by):
@@ -50,7 +64,7 @@
     columns = resid_in.shape[1]
     blocks_dev = enc_weight.shape[2] // BLOCK
     decoders = (
-        lax.all_gather(dec_own[0], "tok", axis=1, tiled=True),
+        meet_surface_over_axis(dec_own[0]),
         lax.all_gather(dec_next[0], "tok", axis=1, tiled=True),
     )
     empty_rows = jnp.zeros((resid_in.shape[0], columns), jnp.bfloat16)

time: 486 us -> 573 us (1.18)
  waiting for transfers between devices: 370 us -> 439 us
  starting transfers between devices: 4 us -> 16.1 us
    all_to_all x0 -> x1, waiting for transfers between devices: none -> 258 us  [wait_pages(): lax.all_to_all(jnp.concatenate([field_in for _ in range(lax.axis_size('to...]
    all_gather x1 -> x0, waiting for transfers between devices: 108 us -> none  [shards(): lax.all_gather(dec_own[0], 'tok', axis=1, tiled=True)]
    all_gather x1, waiting for transfers between devices: 90.5 us -> 0.01 us  [shards(): lax.all_gather(dec_next[0], 'tok', axis=1, tiled=True)]
    all_to_all x0 -> x1, starting transfers between devices: none -> 12.1 us  [wait_pages(): lax.all_to_all(jnp.concatenate([field_in for _ in range(lax.axis_size('to...]
    while x6, waiting for transfers between devices: 161 us -> 172 us
    concatenate x0 -> x1, local copies, waits for them, and re-layouts: none -> 5.83 us  [wait_pages(): jnp.concatenate([field_in for _ in range(lax.axis_size('tok'))], dim_at)]
  transfers between devices with their start and end apart: 8 -> 8, of which waited for: 8 -> 7; matrix products, arithmetic and copies ran while one was open for 3% -> 2% of each run, Pallas kernels for 0% -> 0%
where the time goes in v1:
time: 573 us; the launch traced here: 572 us
  waiting for transfers between devices  439 us (77%)
  local copies, waits for them, and re-layouts  46.7 us (8%)
  blocking collectives  32.2 us (6%)
  matrix products  17.4 us (3%)
  starting transfers between devices  16.1 us (3%)
  between operations  13.8 us (2%)
    all_to_all x1, waiting for transfers between devices, wait_pages(): lax.all_to_all(jnp.concatenate([field_in for _ in range(lax.axis_size('to...  258 us
    while x6, waiting for transfers between devices  172 us
    all_gather x3, blocking collectives, advance(): gathered = lax.all_gather(residual, 'feat', axis=1, tiled=True)  32.2 us
    while x2, local copies, waits for them, and re-layouts, shards(): lax.fori_loop(0, tile_count + layer_count - 1, advance, (nothing_yet, emp...  24.7 us
    all_to_all x1, starting transfers between devices, wait_pages(): lax.all_to_all(jnp.concatenate([field_in for _ in range(lax.axis_size('to...  12.1 us
    dot_general x2, matrix products, decode_every(): jnp.dot(gathered, enc_weight[0], preferred_element_type=jnp.float32)  11.7 us
  transfers between devices with their start and end apart: 8, of which 7 were waited for; matrix products, arithmetic and copies ran while one was open for 2% of the time, Pallas kernels for 0%

profile of v1, /device:TPU:1, one launch (start us, length us, event | category | flops | bytes accessed | tf_op | source)
XLA Modules:
  0.0 571.6 jit_solution(4153172296736090958)
XLA Ops:
  7.2 5.8 %concatenate.7 = bf16[2048,32,72]{0,2,1:T(8,128)(2,1)} broadcast(bf16[2048,72]{0,1:T(8,128)(2,1)} %bitcast.86), dimensions={0,2} | broadcast | bytes 9732096 | tf_op jit(solution)/shard_map/concatenate | solution.py:13
  13.0 12.1 %all-to-all-start = ((bf16[2048,32,72]{0,2,1:T(8,128)(2,1)}), bf16[2048,32,72]{0,2,1:T(8,128)(2,1)}, u32[]{:S(2)}, u32[]{:S(2)}) async-start(bf16[2048,32,72]{0,2,1:T(8,128)(2,1)} %concatenate.7), calls=%async_computation | async-start | bytes 18874368 | tf_op jit(solution)/shard_map/all_to_all | solution.py:12
  25.9 258.2 %all-to-all-done = bf16[2048,32,72]{0,2,1:T(8,128)(2,1)} async-done(((bf16[2048,32,72]{0,2,1:T(8,128)(2,1)}), bf16[2048,32,72]{0,2,1:T(8,128)(2,1)}, u32[]{:S(2)}, u32[]{:S(2)}) %all-to-all-start) | async-done | bytes 9437216 | tf_op jit(solution)/shard_map/all_to_all | solution.py:12
  284.1 12.2 %copy.33 = bf16[2048,2304]{1,0:T(8,128)(2,1)} copy(bf16[2048,2304]{0,1:T(8,128)(2,1)} %bitcast.16) | data formatting | bytes 18874368 | tf_op jit(solution)/shard_map/while | solution.py:109
  296.3 12.6 %copy.34 = bf16[2048,2304]{1,0:T(8,128)(2,1)} copy(bf16[2048,2304]{0,1:T(8,128)(2,1)} %bitcast.83) | data formatting | bytes 18874368 | tf_op jit(solution)/shard_map/while | solution.py:109
  309.1 255.2 %while.19 = (s32[]{:T(128)}, bf16[2,128,576]{1,2,0:T(8,128)(2,1)S(1)}, bf16[256,576]{0,1:T(8,128)(2,1)S(1)}, bf16[256,576]{0,1:T(8,128)(2,1)S(1)}, pred[]{:T(512...) while((s32[]{:T(128)}, ...), condition=%wide.region_5.6_spmd, body=%wide.region_0.5_spmd.sunk | while | flops 3627509248 | bytes 116467488 | solution.py:109
  309.2 10.4 %all_gather.14 = bf16[128,2304]{0,1:T(8,128)(2,1)S(1)} all-gather(bf16[128,576]{0,1:T(8,128)(2,1)S(1)} %bitcast_select_fusion.4), channel_id=1, replica_groups=mesh['layer'=2,'feat'=4,'tok'=32] {'feat'}, dimensions={1}, use_global_device_ids=true | all-gather | bytes 737280 | tf_op jit(solution)/shard_map/while/body/eval_jaxpr/all_gather | solution.py:86
  319.7 2.7 copy.40
  323.7 70.3 %all-reduce.5.cloned.1.call-done = bf16[2,128,2304]{1,0,2:T(2,128)(2,1)} async-done(((bf16[2,128,2304]{1,0,2:T(2,128)(2,1)}), bf16[2,128,2304]{1,0,2:T(2,128)(2,1)}) %all-reduce.5.cloned.1.call-update) | async-done | bytes 1179664 | tf_op jit(solution)/shard_map/while
  394.1 1.2 constant_dynamic-slice_fusion.4
  395.6 1.3 collective-permute-start
  396.9 2.9 collective-permute-done
  399.8 10.9 %all_gather.14 = bf16[128,2304]{0,1:T(8,128)(2,1)S(1)} all-gather(bf16[128,576]{0,1:T(8,128)(2,1)S(1)} %bitcast_select_fusion.4), channel_id=1, replica_groups=mesh['layer'=2,'feat'=4,'tok'=32] {'feat'}, dimensions={1}, use_global_device_ids=true | all-gather | bytes 737280 | tf_op jit(solution)/shard_map/while/body/eval_jaxpr/all_gather | solution.py:86
  410.8 10.8 %conditional.2 = (bf16[2,128,2304]{2,1,0:T(8,128)(2,1)S(1)}) conditional(s32[]{:T(128)} %convert_element_type.137, () %tuple.77, (bf16[1,2304,2048]{2,1,0:T(8,128)(2,1)}, bf16[128,2304]{0,1:T(8,128)(2,1)S(1)}, f32[1,2048]{1,0:T(1,128)S(1)}, s32[1,2,32]{2,1,0:T(2,128)S(1)}, s32[]{:T(128)}, /*index=5*/s32[]{:T(128)}, s32[16,1]{0,1:T(1,128)S(1)}, ...), branch_computations={%region_1.1_spmd, %region_2.3_spmd} | conditional | flops 3625518592 | bytes 100099104 | solution.py:89
  412.6 5.8 %fusion.11 = bf16[128,2048]{1,0:T(8,128)(2,1)S(1)} fusion(bf16[128,2304]{0,1:T(8,128)(2,1)S(1)} %get-tuple-element.519, bf16[1,2304,2048]{2,1,0:T(8,128)(2,1)} %get-tuple-element.426, f32[2048]{0:T(1024)S(1)} %broadcast_bitcast_fusion, f32[2048]{0:T(1024)S(1)} %bitcast.87), kind=kOutput, calls=%fused_computation.7 | convolution fusion | flops 1209008128 | bytes 10567680 | tf_op jit(solution)/shard_map/while/body/eval_jaxpr/cond/branch_1_fun/dot_general | solution.py:41
  418.4 1.4 convolution_bitcast_fusion
  420.0 1.4 convolution_bitcast_fusion.1
  421.6 2.7 copy.40
  425.6 52.3 %all-reduce.5.cloned.1.call-done = bf16[2,128,2304]{1,0,2:T(2,128)(2,1)} async-done(((bf16[2,128,2304]{1,0,2:T(2,128)(2,1)}), bf16[2,128,2304]{1,0,2:T(2,128)(2,1)}) %all-reduce.5.cloned.1.call-update) | async-done | bytes 1179664 | tf_op jit(solution)/shard_map/while
  477.9 1.2 constant_dynamic-slice_fusion.4
  479.5 1.3 collective-permute-start
  480.8 2.9 collective-permute-done
  483.7 10.9 %all_gather.14 = bf16[128,2304]{0,1:T(8,128)(2,1)S(1)} all-gather(bf16[128,576]{0,1:T(8,128)(2,1)S(1)} %bitcast_select_fusion.4), channel_id=1, replica_groups=mesh['layer'=2,'feat'=4,'tok'=32] {'feat'}, dimensions={1}, use_global_device_ids=true | all-gather | bytes 737280 | tf_op jit(solution)/shard_map/while/body/eval_jaxpr/all_gather | solution.py:86
  494.7 10.8 %conditional.2 = (bf16[2,128,2304]{2,1,0:T(8,128)(2,1)S(1)}) conditional(s32[]{:T(128)} %convert_element_type.137, () %tuple.77, (bf16[1,2304,2048]{2,1,0:T(8,128)(2,1)}, bf16[128,2304]{0,1:T(8,128)(2,1)S(1)}, f32[1,2048]{1,0:T(1,128)S(1)}, s32[1,2,32]{2,1,0:T(2,128)S(1)}, s32[]{:T(128)}, /*index=5*/s32[]{:T(128)}, s32[16,1]{0,1:T(1,128)S(1)}, ...), branch_computations={%region_1.1_spmd, %region_2.3_spmd} | conditional | flops 3625518592 | bytes 100099104 | solution.py:89
  496.5 5.8 %fusion.11 = bf16[128,2048]{1,0:T(8,128)(2,1)S(1)} fusion(bf16[128,2304]{0,1:T(8,128)(2,1)S(1)} %get-tuple-element.519, bf16[1,2304,2048]{2,1,0:T(8,128)(2,1)} %get-tuple-element.426, f32[2048]{0:T(1024)S(1)} %broadcast_bitcast_fusion, f32[2048]{0:T(1024)S(1)} %bitcast.87), kind=kOutput, calls=%fused_computation.7 | convolution fusion | flops 1209008128 | bytes 10567680 | tf_op jit(solution)/shard_map/while/body/eval_jaxpr/cond/branch_1_fun/dot_general | solution.py:41
  502.3 1.4 convolution_bitcast_fusion
  503.9 1.4 convolution_bitcast_fusion.1
  505.4 2.7 copy.40
  509.5 49.0 %all-reduce.5.cloned.1.call-done = bf16[2,128,2304]{1,0,2:T(2,128)(2,1)} async-done(((bf16[2,128,2304]{1,0,2:T(2,128)(2,1)}), bf16[2,128,2304]{1,0,2:T(2,128)(2,1)}) %all-reduce.5.cloned.1.call-update) | async-done | bytes 1179664 | tf_op jit(solution)/shard_map/while
  558.5 1.2 constant_dynamic-slice_fusion.4
  560.0 1.3 collective-permute-start
  561.3 2.9 collective-permute-done
  (90 shorter events, 9.0 us)
Async XLA Ops:
  13.0 271.1 %all-to-all-start = ((bf16[2048,32,72]{0,2,1:T(8,128)(2,1)}), bf16[2048,32,72]{0,2,1:T(8,128)(2,1)}, u32[]{:S(2)}, u32[]{:S(2)}) async-start(bf16[2048,32,72]{0,2,1:T(8,128)(2,1)} %concatenate.7), calls=%async_computation | async-start | bytes 18874368 | tf_op jit(solution)/shard_map/all_to_all | solution.py:12
  25.1 271.1 %all-gather.3.cloned.1.call-start = ((), (), s32[]{:S(2)}) async-start(), calls=%async_computation.1 | async-start | bytes 9732096 | tf_op jit(solution)/shard_map/all_gather | solution.py:68
  296.3 12.7 %copy-start.1 = (bf16[256,576]{0,1:T(8,128)(2,1)S(1)}, bf16[256,576]{0,1:T(8,128)(2,1)}, u32[]{:S(2)}) copy-start(bf16[256,576]{0,1:T(8,128)(2,1)} %param.15) | copy-start | bytes 884740
  296.3 12.7 %copy-start.4 = (bf16[1,256,576]{1,2,0:T(8,128)(2,1)S(1)}, bf16[1,256,576]{1,2,0:T(8,128)(2,1)}, u32[]{:S(2)}) copy-start(bf16[1,256,576]{1,2,0:T(8,128)(2,1)} %param.14) | copy-start | bytes 884740
  296.3 12.7 %copy-start.5 = (bf16[256,576]{0,1:T(8,128)(2,1)S(1)}, bf16[256,576]{0,1:T(8,128)(2,1)}, u32[]{:S(2)}) copy-start(bf16[256,576]{0,1:T(8,128)(2,1)} %param.13) | copy-start | bytes 884740
  296.3 12.8 %copy-start.6 = (f32[1,2048]{1,0:T(1,128)S(1)}, f32[1,2048]{1,0:T(1,128)}, u32[]{:S(2)}) copy-start(f32[1,2048]{1,0:T(1,128)} %param.17) | copy-start | bytes 24580
  296.3 12.7 %copy-start.7 = (s32[1,2,32]{2,1,0:T(2,128)S(1)}, s32[1,2,32]{2,1,0:T(2,128)}, u32[]{:S(2)}) copy-start(s32[1,2,32]{2,1,0:T(2,128)} %param.20) | copy-start | bytes 772
  296.3 12.7 %copy-start.8 = (s32[1,2]{1,0:T(1,128)S(1)}, s32[1,2]{1,0:T(1,128)}, u32[]{:S(2)}) copy-start(s32[1,2]{1,0:T(1,128)} %param.21) | copy-start | bytes 28
  296.3 12.7 %copy-start.9 = (u32[256]{0:T(256)S(1)}, u32[256]{0:T(256)}, u32[]{:S(2)}) copy-start(u32[256]{0:T(256)} %constant.151) | copy-start | bytes 3076
  309.1 85.0 %all-reduce.5.cloned.1.call-start = ((), (), s32[]{:S(2)}) async-start(), calls=%async_computation.2 | async-start | bytes 2359296 | tf_op jit(solution)/shard_map/while
  395.6 4.2 collective-permute-start
  399.8 78.1 %all-reduce.5.cloned.1.call-start = ((), (), s32[]{:S(2)}) async-start(), calls=%async_computation.2 | async-start | bytes 2359296 | tf_op jit(solution)/shard_map/while
  410.8 7.6 %copy-start = (bf16[2048,2304]{1,0:T(8,128)(2,1)S(1)}, bf16[2048,2304]{1,0:T(8,128)(2,1)}, u32[]{:S(2)}) copy-start(bf16[2048,2304]{1,0:T(8,128)(2,1)} %get-tuple-element.435) | copy-start | bytes 28311556 | tf_op jit(solution)/shard_map/while/body/eval_jaxpr/cond
  412.6 7.3 %slice-start = ((s8[9437184]{0:T(1024)(128)(4,1)}), s8[4194304]{0:T(1024)(128)(4,1)S(1)}, s32[]{:S(2)}) async-start(s8[9437184]{0:T(1024)(128)(4,1)} %bitcast.81), calls=%async_computation.3 | async-start | bytes 8388608 | tf_op jit(solution)/shard_map/while/body/eval_jaxpr/cond
  412.6 7.3 %slice-start.1 = ((s8[9437184]{0:T(1024)(128)(4,1)}), s8[4194304]{0:T(1024)(128)(4,1)S(1)}, s32[]{:S(2)}) async-start(s8[9437184]{0:T(1024)(128)(4,1)} %bitcast.81), calls=%async_computation.4 | async-start | bytes 8388608 | tf_op jit(solution)/shard_map/while/body/eval_jaxpr/cond
  418.4 1.6 slice-start.2
  479.5 4.2 collective-permute-start
  483.7 74.8 %all-reduce.5.cloned.1.call-start = ((), (), s32[]{:S(2)}) async-start(), calls=%async_computation.2 | async-start | bytes 2359296 | tf_op jit(solution)/shard_map/while
  494.7 7.6 %copy-start = (bf16[2048,2304]{1,0:T(8,128)(2,1)S(1)}, bf16[2048,2304]{1,0:T(8,128)(2,1)}, u32[]{:S(2)}) copy-start(bf16[2048,2304]{1,0:T(8,128)(2,1)} %get-tuple-element.435) | copy-start | bytes 28311556 | tf_op jit(solution)/shard_map/while/body/eval_jaxpr/cond
  496.5 7.3 %slice-start = ((s8[9437184]{0:T(1024)(128)(4,1)}), s8[4194304]{0:T(1024)(128)(4,1)S(1)}, s32[]{:S(2)}) async-start(s8[9437184]{0:T(1024)(128)(4,1)} %bitcast.81), calls=%async_computation.3 | async-start | bytes 8388608 | tf_op jit(solution)/shard_map/while/body/eval_jaxpr/cond
  496.5 7.3 %slice-start.1 = ((s8[9437184]{0:T(1024)(128)(4,1)}), s8[4194304]{0:T(1024)(128)(4,1)S(1)}, s32[]{:S(2)}) async-start(s8[9437184]{0:T(1024)(128)(4,1)} %bitcast.81), calls=%async_computation.4 | async-start | bytes 8388608 | tf_op jit(solution)/shard_map/while/body/eval_jaxpr/cond
  502.3 1.6 slice-start.2
  560.0 4.2 collective-permute-start
  564.2 0.7 copy-start.2
  564.2 0.8 copy-start.3
Sparse Core Ops, SparseCore 0:
  28.5 243.1 all-gather.2
  322.5 71.5 all-reduce.4
  424.4 53.4 all-reduce.4
  508.3 50.1 all-reduce.4
